TPU v7x, 32 devices: a whole 2x2x4 slice. The times are simulated.
32 devices in a mesh: tok: 8 (over z, x), grp: 4 (over y, core).
Axes of the slice: x: 2, y: 2, z: 4, core: 2. Of those that a mesh axis runs over, the one named last changes fastest.
Arguments:
- queries: bfloat16 [1536, 2048], P('tok', 'grp'), may hold values from -72 to 72
- new_keys: bfloat16 [1536, 2048], P('tok', 'grp'), may hold values from -8 to 8
- new_values: bfloat16 [1536, 2048], P('tok', 'grp'), may hold values from -6 to 6
- residual: bfloat16 [1536, 2048], P('tok', 'grp'), may hold values from -6 to 6
- w_out: bfloat16 [2048, 2048], P('grp'), may hold values from -0.125 to 0.125
- leaf_keys: bfloat16 [8, 512, 2048], P('tok', None, 'grp'), may hold values from -6 to 6
- leaf_values: bfloat16 [8, 512, 2048], P('tok', None, 'grp'), may hold values from -6 to 6
- upper_keys: bfloat16 [6, 1024, 2048], P(None, 'tok', 'grp'), may hold values from -8 to 8
- upper_values: bfloat16 [6, 1024, 2048], P(None, 'tok', 'grp'), may hold values from -6 to 6
- req_len: int32 [8], replicated, may hold values from 48 to 192, as said below
- leaf_mid: int32 [8], replicated, may hold values from 0 to 3
- mid_root: int32 [4], replicated, may hold values from 0 to 1, as said below
- upper_len: int32 [6], replicated, may hold values from 256 to 1024, as said below
- leaf_len: int32 [8], replicated, may hold values from 128 to 512, as said below
Outputs:
- hidden_out: bfloat16 [1536, 2048], P('tok', 'grp')
Inputs may be any that keep to these rules, and one draw needn't show every extreme that they name: `req_len`: some request has exactly 192 new tokens. `mid_root`: each root is the parent of 2 mids. `upper_len`: the first 2 entries are roots and equal 1024. `leaf_len`: some leaf has exactly 512 positions.
All inputs are finite; a program needn't handle non-finite values.
Results may differ from a plain program's by a relative error of at most 0.008.
Values may be sent and summed in bfloat16 or wider, within the bound.
No kernel may reach another device: no remote copies, remote signals or barrier semaphores. Data moves between devices by JAX's collectives and lax.ppermute only.
A program may use at most 64 MiB of HBM per device.

v0:
```python
import math
import jax
import jax.numpy as jnp
from jax import lax
from jax.sharding import PartitionSpec as P

HEAD_DIM = 128
NEG_FILL = -1e30


def partial_attention(query_rows, key_rows, values, allowed, head_count):
    head_width = query_rows.shape[1] // head_count
    query_heads = query_rows.reshape(query_rows.shape[0], head_count, head_width)
    key_heads = key_rows.reshape(key_rows.shape[0], head_count, head_width)
    value_heads = values.reshape(values.shape[0], head_count, head_width)
    scores = jnp.einsum(
        "qhd,khd->hqk", query_heads, key_heads, preferred_element_type=jnp.float32
    ) * head_width ** (-0.5)
    scores = jnp.where(allowed[None], scores, NEG_FILL)
    row_max = jnp.max(scores, axis=2)
    exp_scores = jnp.where(allowed[None], jnp.exp(scores - row_max[:, :, None]), 0.0)
    row_total = jnp.sum(exp_scores, axis=2)
    weighted = jnp.einsum(
        "hqk,khd->hqd",
        exp_scores.astype(jnp.bfloat16),
        value_heads,
        preferred_element_type=jnp.float32,
    )
    return (row_max, row_total, weighted)


def combine(earlier, latter):
    new_max = jnp.maximum(earlier[0], latter[0])
    earlier_scale = jnp.exp(earlier[0] - new_max)
    latter_scale = jnp.exp(latter[0] - new_max)
    return (
        new_max,
        earlier[1] * earlier_scale + latter[1] * latter_scale,
        earlier[2] * earlier_scale[:, :, None] + latter[2] * latter_scale[:, :, None],
    )


def node_attention(carry, query_rows, node_keys, node_values, node_len, head_count):
    node_rows = node_keys.shape[0]
    block = math.gcd(node_rows, 512)
    row_count = query_rows.shape[0]
    for start in range(0, node_rows, block):
        positions = start + jnp.arange(block, dtype=jnp.int32)
        allowed = jnp.broadcast_to((positions < node_len)[None, :], (row_count, block))
        piece_part = partial_attention(
            query_rows,
            node_keys[start : start + block],
            node_values[start : start + block],
            allowed,
            head_count,
        )
        carry = combine(carry, piece_part)
    return carry


def shards(
    queries,
    new_keys,
    new_values,
    residual,
    w_out,
    leaf_keys,
    leaf_values,
    upper_keys,
    upper_values,
    req_len,
    leaf_mid,
    mid_root,
    upper_len,
    leaf_len,
):
    dev_count = lax.axis_size("tok")
    my_index = lax.axis_index("tok")
    row_count = queries.shape[0]
    col_count = queries.shape[1]
    head_count = col_count // HEAD_DIM
    mid_count = mid_root.shape[0]
    node_count = upper_len.shape[0]
    root_count = node_count - mid_count
    owned = (jnp.arange(dev_count, dtype=jnp.int32) == my_index).astype(jnp.int32)
    my_length = jnp.sum(owned * req_len)
    my_mid = jnp.sum(owned * leaf_mid)
    my_leaf_len = jnp.sum(owned * leaf_len)
    my_root = jnp.sum((jnp.arange(mid_count) == my_mid).astype(jnp.int32) * mid_root)
    node_ids = jnp.arange(node_count)
    root_len = jnp.sum((node_ids == my_root).astype(jnp.int32) * upper_len)
    mid_len = jnp.sum((node_ids == root_count + my_mid).astype(jnp.int32) * upper_len)
    position = jnp.arange(row_count, dtype=jnp.int32)
    is_live = position < my_length
    leaf_count = leaf_keys.shape[1]
    local_keys = jnp.concatenate([leaf_keys[0], new_keys], axis=0)
    local_values = jnp.concatenate([leaf_values[0], new_values], axis=0)
    leaf_allowed = jnp.broadcast_to(
        (jnp.arange(leaf_count) < my_leaf_len)[None, :], (row_count, leaf_count)
    )
    new_allowed = (position[None, :] <= position[:, None]) & is_live[None, :]
    local_part = partial_attention(
        queries,
        local_keys,
        local_values,
        jnp.concatenate([leaf_allowed, new_allowed], axis=1),
        head_count,
    )
    gathered_keys, gathered_values = (
        lax.all_gather(upper_keys, "tok", axis=1, tiled=True),
        lax.all_gather(upper_values, "tok", axis=1, tiled=True),
    )
    merged = node_attention(
        local_part, queries, gathered_keys[my_root], gathered_values[my_root], root_len, head_count
    )
    merged = node_attention(
        merged,
        queries,
        gathered_keys[root_count + my_mid],
        gathered_values[root_count + my_mid],
        mid_len,
        head_count,
    )
    attended = (merged[2] / merged[1][:, :, None]).transpose(1, 0, 2).reshape(row_count, col_count)
    attention = jnp.where(is_live[:, None], attended, 0.0).astype(jnp.bfloat16)
    projected = jnp.dot(attention, w_out, preferred_element_type=jnp.float32)
    mixed = lax.psum_scatter(
        projected.astype(jnp.bfloat16), "grp", scatter_dimension=1, tiled=True
    ).astype(jnp.float32)
    return (residual.astype(jnp.float32) + mixed).astype(jnp.bfloat16)


def solution(mesh):
    in_specs = (
        P("tok", "grp"),
        P("tok", "grp"),
        P("tok", "grp"),
        P("tok", "grp"),
        P("grp", None),
        P("tok", None, "grp"),
        P("tok", None, "grp"),
        P(None, "tok", "grp"),
        P(None, "tok", "grp"),
        P(),
        P(),
        P(),
        P(),
        P(),
    )
    out_specs = P("tok", "grp")
    return jax.shard_map(shards, mesh=mesh, in_specs=in_specs, out_specs=out_specs, check_vma=False)
```

profile of v0, /device:TPU:0, one launch (start us, length us, event | category | flops | bytes accessed | tf_op | source)
XLA Modules:
  0.0 251.3 jit_solution(10677370438847150841)
XLA Ops:
  6.5 2.5 copy.27
  9.1 1.2 copy.30
  12.3 1.3 fusion.91
  15.1 1.0 copy.21
  16.2 1.3 copy.24
  18.9 1.2 fusion.92
  21.4 0.7 fusion.90
  22.0 0.7 iota_compare_fusion.2
  23.3 0.6 iota_compare_fusion.4
  24.1 1.0 copy_bitcast_fusion
  25.1 1.7 fusion
  26.9 1.4 copy-done.10
  28.3 0.9 fusion.1
  29.1 82.9 %all-gather.3.cloned.1.call-done = bf16[6,1024,512]{1,2,0:T(8,128)(2,1)} async-done(((bf16[6,128,512]{1,2,0:T(8,128)(2,1)}), bf16[6,1024,512]{1,2,0:T(8,128)(2,1)}) %all-gather.3.cloned.1.call-update) | async-done | bytes 6291472 | tf_op jit(solution)/shard_map/all_gather | solution.py:110
  112.1 1.7 constant_dynamic-slice_fusion.3
  117.7 1.1 copy-done.7
  119.4 92.8 %all-gather.5.cloned.1.call-done = bf16[6,1024,512]{1,2,0:T(8,128)(2,1)} async-done(((bf16[6,128,512]{1,2,0:T(8,128)(2,1)}), bf16[6,1024,512]{1,2,0:T(8,128)(2,1)}) %all-gather.5.cloned.1.call-update) | async-done | bytes 6291472 | tf_op jit(solution)/shard_map/all_gather | solution.py:111
  212.3 1.8 constant_dynamic-slice_fusion.4
  214.8 0.7 copy-done.8
  216.6 1.0 fusion.31
  218.5 0.8 copy-done.4
  219.9 1.5 convolution_convert_fusion
  221.4 21.6 %reduce-scatter.2.cloned.1.call-done = bf16[192,512]{1,0:T(8,128)(2,1)} async-done(((bf16[192,2048]{1,0:T(8,128)(2,1)}), bf16[192,512]{1,0:T(8,128)(2,1)}) %reduce-scatter.2.cloned.1.call-update) | async-done | bytes 196624 | tf_op jit(solution)/shard_map/reduce_scatter | solution.py:127
  243.1 1.7 add_convert_fusion
  (68 shorter events, 11.6 us)
Async XLA Ops:
  6.5 213.3 %copy-start = (bf16[512,2048]{1,0:T(8,128)(2,1)S(1)}, bf16[512,2048]{1,0:T(8,128)(2,1)}, u32[]{:S(2)}) copy-start(bf16[512,2048]{1,0:T(8,128)(2,1)} %param.18) | copy-start | bytes 6291460
  6.5 2.6 %copy-start.12 = (bf16[6,128,512]{2,1,0:T(8,128)(2,1)S(1)}, bf16[6,128,512]{2,1,0:T(8,128)(2,1)}, u32[]{:S(2)}) copy-start(bf16[6,128,512]{2,1,0:T(8,128)(2,1)} %param.22) | copy-start | bytes 2359300
  6.5 105.5 %all-gather.3.cloned.1.call-start = ((), (), s32[]{:S(2)}) async-start(), calls=%async_computation.1 | async-start | bytes 7077888 | tf_op jit(solution)/shard_map/all_gather | solution.py:110
  9.0 1.3 copy-start.16
  9.0 1.4 copy-start.17
  9.0 3.3 %copy-start.19 = (s32[4]{0:T(128)S(1)}, s32[4]{0:T(128)}, u32[]{:S(2)}) copy-start(s32[4]{0:T(128)} %param.25) | copy-start | bytes 52
  9.0 5.8 %copy-start.13 = (bf16[1,512,512]{2,1,0:T(8,128)(2,1)S(1)}, bf16[1,512,512]{2,1,0:T(8,128)(2,1)}, u32[]{:S(2)}) copy-start(bf16[1,512,512]{2,1,0:T(8,128)(2,1)} %param.19) | copy-start | bytes 1572868
  9.0 203.2 %all-gather.5.cloned.1.call-start = ((), (), s32[]{:S(2)}) async-start(), calls=%async_computation.2 | async-start | bytes 7077888 | tf_op jit(solution)/shard_map/all_gather | solution.py:111
  10.3 232.8 %reduce-scatter.2.cloned.1.call-start = ((), (), s32[]{:S(2)}) async-start(), calls=%async_computation.3 | async-start | bytes 983040 | tf_op jit(solution)/shard_map/reduce_scatter | solution.py:127
  15.1 3.9 %copy-start.18 = (s32[6]{0:T(128)S(1)}, s32[6]{0:T(128)}, u32[]{:S(2)}) copy-start(s32[6]{0:T(128)} %param.26) | copy-start | bytes 76
  15.1 7.6 %copy-start.20 = (s32[8]{0:T(128)S(1)}, s32[8]{0:T(128)}, u32[]{:S(2)}) copy-start(s32[8]{0:T(128)} %param.23) | copy-start | bytes 100
  15.1 9.0 %copy-start.14 = (bf16[192,512]{1,0:T(8,128)(2,1)S(1)}, bf16[192,512]{1,0:T(8,128)(2,1)}, u32[]{:S(2)}) copy-start(bf16[192,512]{1,0:T(8,128)(2,1)} %param.15) | copy-start | bytes 589828
  16.2 8.9 %copy-start.9 = (bf16[192,512]{1,0:T(8,128)(2,1)S(1)}, bf16[192,512]{1,0:T(8,128)(2,1)}, u32[]{:S(2)}) copy-start(bf16[192,512]{1,0:T(8,128)(2,1)} %param.14) | copy-start | bytes 589828
  26.8 1.4 copy-start.10
  114.2 1.2 copy-start.3
  115.3 1.2 copy-start.5
  116.5 1.2 copy-start.1
  117.7 1.1 copy-start.7
  212.3 2.0 copy-start.6
  214.0 1.5 copy-start.8
  214.8 1.8 copy-start.11
  216.6 1.4 copy-start.2
  218.0 1.4 copy-start.4
  219.9 23.2 %copy-start.15 = (bf16[192,512]{1,0:T(8,128)(2,1)S(1)}, bf16[192,512]{1,0:T(8,128)(2,1)}, u32[]{:S(2)}) copy-start(bf16[192,512]{1,0:T(8,128)(2,1)} %param.17) | copy-start | bytes 589828
Sparse Core Ops, SparseCore 0:
  9.4 102.6 all-gather.2
  114.1 98.1 all-gather.4
  221.6 21.4 reduce-scatter.1
where the time goes:
time: 252 us; the launch traced here: 251 us
  waiting for transfers between devices  197 us (78%)
  local copies, waits for them, and re-layouts  16.9 us (7%)
  between operations  16.5 us (7%)
  other arithmetic  12.3 us (5%)
  matrix products  8.03 us (3%)
    all_gather x1, waiting for transfers between devices, shards(): lax.all_gather(upper_values, 'tok', axis=1, tiled=True)  92.8 us
    all_gather x1, waiting for transfers between devices, shards(): lax.all_gather(upper_keys, 'tok', axis=1, tiled=True)  82.9 us
    reduce_scatter x1, waiting for transfers between devices, shards(): lax.psum_scatter(projected.astype(jnp.bfloat16), 'grp', scatter_dimension...  21.6 us
    unnamed x46, local copies, waits for them, and re-layouts  11.2 us
  transfers between devices with their start and end apart: 3, of which 3 were waited for; matrix products, arithmetic and copies ran while one was open for 8% of the time, Pallas kernels for 0%

commit v1 on v0

--- a/solution.py
+++ b/solution.py
@@ -6,6 +6,18 @@
 
 HEAD_DIM = 128
 NEG_FILL = -1e30
+
+
+def gather_by_bits(x, axis, dim):
+    ways, here = (lax.axis_size(axis), lax.axis_index(axis))
+    grown, reach = (x, 1)
+    while reach < ways:
+        theirs = lax.ppermute(grown, axis, [(d, d ^ reach) for d in range(ways)])
+        mine_first = jnp.concatenate([grown, theirs], axis=dim)
+        theirs_first = jnp.concatenate([theirs, grown], axis=dim)
+        grown = jnp.where(here & reach == 0, mine_first, theirs_first)
+        reach = 2 * reach
+    return grown
 
 
 def partial_attention(query_rows, key_rows, values, allowed, head_count):
@@ -107,7 +119,7 @@
         head_count,
     )
     gathered_keys, gathered_values = (
-        lax.all_gather(upper_keys, "tok", axis=1, tiled=True),
+        gather_by_bits(upper_keys, "tok", 1),
         lax.all_gather(upper_values, "tok", axis=1, tiled=True),
     )
     merged = node_attention(

time: 252 us -> 333 us (1.32)
  waiting for transfers between devices: 197 us -> 260 us
  other arithmetic: 12.3 us -> 27.4 us
  starting transfers between devices: 0.09 us -> 5.35 us
    ppermute x0 -> x3, waiting for transfers between devices: none -> 238 us  [gather_by_bits(): theirs = lax.ppermute(grown, axis, [(d, d ^ reach) for d in range(ways)])]
    all_gather x1, waiting for transfers between devices: 92.8 us -> 0.02 us  [shards(): lax.all_gather(upper_values, 'tok', axis=1, tiled=True)]
    all_gather x1 -> x0, waiting for transfers between devices: 82.9 us -> none  [shards(): lax.all_gather(upper_keys, 'tok', axis=1, tiled=True)]
    select_n x0 -> x3, other arithmetic: none -> 15.2 us  [gather_by_bits(): grown = jnp.where(here & reach == 0, mine_first, theirs_first)]
    ppermute x0 -> x3, starting transfers between devices: none -> 5.3 us  [gather_by_bits(): theirs = lax.ppermute(grown, axis, [(d, d ^ reach) for d in range(ways)])]
    unnamed x46 -> x44, local copies, waits for them, and re-layouts: 11.2 us -> 10.6 us
  transfers between devices with their start and end apart: 3 -> 5, of which waited for: 3 -> 4; matrix products, arithmetic and copies ran while one was open for 8% -> 11% of each run, Pallas kernels for 0% -> 0%
where the time goes in v1:
time: 333 us; the launch traced here: 332 us
  waiting for transfers between devices  260 us (78%)
  other arithmetic  27.4 us (8%)
  between operations  16.9 us (5%)
  local copies, waits for them, and re-layouts  14.9 us (4%)
  matrix products  8.02 us (2%)
  starting transfers between devices  5.35 us (2%)
    ppermute x3, waiting for transfers between devices, gather_by_bits(): theirs = lax.ppermute(grown, axis, [(d, d ^ reach) for d in range(ways)])  238 us
    reduce_scatter x1, waiting for transfers between devices, shards(): lax.psum_scatter(projected.astype(jnp.bfloat16), 'grp', scatter_dimension...  21.1 us
    select_n x3, other arithmetic, gather_by_bits(): grown = jnp.where(here & reach == 0, mine_first, theirs_first)  15.2 us
    unnamed x44, local copies, waits for them, and re-layouts  10.6 us
  transfers between devices with their start and end apart: 5, of which 4 were waited for; matrix products, arithmetic and copies ran while one was open for 11% of the time, Pallas kernels for 0%

profile of v1, /device:TPU:0, one launch (start us, length us, event | category | flops | bytes accessed | tf_op | source)
XLA Modules:
  0.0 332.2 jit_solution(11666580835793956953)
XLA Ops:
  6.5 2.4 copy.32
  9.1 1.5 copy.28
  10.6 3.0 collective-permute-start
  13.6 26.1 %collective-permute-done = bf16[6,128,512]{1,2,0:T(8,128)(2,1)} collective-permute-done((bf16[6,128,512]{1,2,0:T(8,128)(2,1)S(1)}, bf16[6,128,512]{1,2,0:T(8,128)(2,1)}, u32[]{:S(2)}, u32[]{:S(2)}) %collective-permute-start) | collective-permute-done | bytes 786464 | tf_op jit(solution)/shard_map/ppermute | solution.py:15
  39.7 3.1 maximum_select_fusion.2
  42.7 1.8 collective-permute-start.1
  44.6 69.3 %collective-permute-done.1 = bf16[6,256,512]{1,2,0:T(8,128)(2,1)} collective-permute-done((bf16[6,256,512]{1,2,0:T(8,128)(2,1)}, bf16[6,256,512]{1,2,0:T(8,128)(2,1)}, u32[]{:S(2)}, u32[]{:S(2)}) %collective-permute-start.1) | collective-permute-done | bytes 1572896 | tf_op jit(solution)/shard_map/ppermute | solution.py:15
  113.9 4.9 %maximum_select_fusion.1 = bf16[6,512,512]{1,2,0:T(8,128)(2,1)} fusion(bf16[6,256,512]{1,2,0:T(8,128)(2,1)} %collective-permute-done.1, bf16[6,256,512]{1,2,0:T(8,128)(2,1)} %maximum_select_fusion.2, pred[]{:T(512)S(6)} %eq.40), kind=kLoop, calls=%fused_computation.1 | loop fusion | flops 14155776 | bytes 6291457 | tf_op jit(solution)/shard_map/jit(_where)/select_n | solution.py:18
  121.2 1.3 fusion.91
  124.0 1.0 copy.21
  125.0 1.3 copy.24
  127.8 1.2 fusion.92
  133.0 1.0 copy_bitcast_fusion
  134.0 1.7 fusion
  135.7 0.9 fusion.1
  137.2 143.0 %collective-permute-done.2 = bf16[6,512,512]{1,2,0:T(8,128)(2,1)} collective-permute-done((bf16[6,512,512]{1,2,0:T(8,128)(2,1)}, bf16[6,512,512]{1,2,0:T(8,128)(2,1)}, u32[]{:S(2)}, u32[]{:S(2)}) %collective-permute-start.2) | collective-permute-done | bytes 3145760 | tf_op jit(solution)/shard_map/ppermute | solution.py:15
  280.2 7.2 %maximum_select_fusion = bf16[6,1024,512]{1,2,0:T(8,128)(2,1)S(1)} fusion(bf16[6,512,512]{1,2,0:T(8,128)(2,1)} %collective-permute-done.2, bf16[6,512,512]{1,2,0:T(8,128)(2,1)} %maximum_select_fusion.1, pred[]{:T(512)S(6)} %eq.39), kind=kLoop, calls=%fused_computation | loop fusion | flops 28311552 | bytes 12582913 | tf_op jit(solution)/shard_map/jit(_where)/select_n | solution.py:18
  291.7 1.1 copy-done.7
  293.4 1.8 constant_dynamic-slice_fusion.4
  297.7 1.0 fusion.31
  299.6 0.8 copy-done.4
  301.0 1.5 convolution_convert_fusion
  302.6 21.1 %reduce-scatter.2.cloned.1.call-done = bf16[192,512]{1,0:T(8,128)(2,1)} async-done(((bf16[192,2048]{1,0:T(8,128)(2,1)}), bf16[192,512]{1,0:T(8,128)(2,1)}) %reduce-scatter.2.cloned.1.call-update) | async-done | bytes 196624 | tf_op jit(solution)/shard_map/reduce_scatter | solution.py:139
  323.7 1.7 add_convert_fusion
  (72 shorter events, 15.5 us)
Async XLA Ops:
  6.5 294.5 %copy-start = (bf16[512,2048]{1,0:T(8,128)(2,1)S(1)}, bf16[512,2048]{1,0:T(8,128)(2,1)}, u32[]{:S(2)}) copy-start(bf16[512,2048]{1,0:T(8,128)(2,1)} %param.18) | copy-start | bytes 6291460
  6.5 286.8 %all-gather.2.cloned.1.call-start = ((), (), s32[]{:S(2)}) async-start(), calls=%async_computation.1 | async-start | bytes 7077888 | tf_op jit(solution)/shard_map/all_gather | solution.py:123
  9.0 314.7 %reduce-scatter.2.cloned.1.call-start = ((), (), s32[]{:S(2)}) async-start(), calls=%async_computation.2 | async-start | bytes 983040 | tf_op jit(solution)/shard_map/reduce_scatter | solution.py:139
  10.6 29.1 %collective-permute-start = (bf16[6,128,512]{1,2,0:T(8,128)(2,1)S(1)}, bf16[6,128,512]{1,2,0:T(8,128)(2,1)}, u32[]{:S(2)}, u32[]{:S(2)}) collective-permute-start(bf16[6,128,512]{1,2,0:T(8,128)(2,1)S(1)} %copy.28), channel_id=1, source_target_pairs={{0,4},{4,0},{8,12},{12,8},{16,20},{20,16},{24,28},{28,24},{1,5},{5... | collective-permute-start | bytes 2359304 | tf_op jit(solution)/shard_map/ppermute | solution.py:15
  42.7 71.2 %collective-permute-start.1 = (bf16[6,256,512]{1,2,0:T(8,128)(2,1)}, bf16[6,256,512]{1,2,0:T(8,128)(2,1)}, u32[]{:S(2)}, u32[]{:S(2)}) collective-permute-start(bf16[6,256,512]{1,2,0:T(8,128)(2,1)} %maximum_select_fusion.2), channel_id=1, source_target_pairs={{0,8},{4,12},{8,0},{12,4},{16,24},{20,28},{24,16},{28,20},{1,9},{5... | collective-permute-start | bytes 4718600 | tf_op jit(solution)/shard_map/ppermute | solution.py:15
  44.6 74.7 %copy-start.15 = (s32[8]{0:T(128)S(1)}, s32[8]{0:T(128)}, u32[]{:S(2)}) copy-start(s32[8]{0:T(128)} %param.24) | copy-start | bytes 100
  44.6 74.7 %copy-start.16 = (s32[8]{0:T(128)S(1)}, s32[8]{0:T(128)}, u32[]{:S(2)}) copy-start(s32[8]{0:T(128)} %param.27) | copy-start | bytes 100
  44.6 76.6 %copy-start.18 = (s32[4]{0:T(128)S(1)}, s32[4]{0:T(128)}, u32[]{:S(2)}) copy-start(s32[4]{0:T(128)} %param.25) | copy-start | bytes 52
  44.6 79.2 %copy-start.12 = (bf16[1,512,512]{2,1,0:T(8,128)(2,1)S(1)}, bf16[1,512,512]{2,1,0:T(8,128)(2,1)}, u32[]{:S(2)}) copy-start(bf16[1,512,512]{2,1,0:T(8,128)(2,1)} %param.19) | copy-start | bytes 1572868
  118.8 161.4 %collective-permute-start.2 = (bf16[6,512,512]{1,2,0:T(8,128)(2,1)}, bf16[6,512,512]{1,2,0:T(8,128)(2,1)}, u32[]{:S(2)}, u32[]{:S(2)}) collective-permute-start(bf16[6,512,512]{1,2,0:T(8,128)(2,1)} %maximum_select_fusion.1), channel_id=1, source_target_pairs={{0,16},{4,20},{8,24},{12,28},{16,0},{20,4},{24,8},{28,12},{1,17},{... | collective-permute-start | bytes 9437192 | tf_op jit(solution)/shard_map/ppermute | solution.py:15
  124.0 3.9 %copy-start.17 = (s32[6]{0:T(128)S(1)}, s32[6]{0:T(128)}, u32[]{:S(2)}) copy-start(s32[6]{0:T(128)} %param.26) | copy-start | bytes 76
  124.0 7.6 %copy-start.19 = (s32[8]{0:T(128)S(1)}, s32[8]{0:T(128)}, u32[]{:S(2)}) copy-start(s32[8]{0:T(128)} %param.23) | copy-start | bytes 100
  124.0 9.0 %copy-start.13 = (bf16[192,512]{1,0:T(8,128)(2,1)S(1)}, bf16[192,512]{1,0:T(8,128)(2,1)}, u32[]{:S(2)}) copy-start(bf16[192,512]{1,0:T(8,128)(2,1)} %param.15) | copy-start | bytes 589828
  125.0 8.9 %copy-start.9 = (bf16[192,512]{1,0:T(8,128)(2,1)S(1)}, bf16[192,512]{1,0:T(8,128)(2,1)}, u32[]{:S(2)}) copy-start(bf16[192,512]{1,0:T(8,128)(2,1)} %param.14) | copy-start | bytes 589828
  135.7 1.4 copy-start.10
  288.1 1.2 copy-start.3
  289.2 1.2 copy-start.5
  290.4 1.2 copy-start.1
  293.4 2.0 copy-start.6
  295.2 1.5 copy-start.8
  295.9 1.8 copy-start.11
  297.7 1.4 copy-start.2
  299.1 1.4 copy-start.4
  301.0 22.7 %copy-start.14 = (bf16[192,512]{1,0:T(8,128)(2,1)S(1)}, bf16[192,512]{1,0:T(8,128)(2,1)}, u32[]{:S(2)}) copy-start(bf16[192,512]{1,0:T(8,128)(2,1)} %param.17) | copy-start | bytes 589828
  (1 other events, 1.1 us)
Sparse Core Ops, SparseCore 0:
  9.4 219.2 all-gather.1
  302.7 20.9 reduce-scatter.1
